TPU v7x, 512 devices: a whole 4x8x8 slice. The times are simulated.
512 devices in a mesh: seq: 16 (over z, core), mlp: 8 (over y), tp: 4 (over x).
Axes of the slice: x: 4, y: 8, z: 8, core: 2. Of those that a mesh axis runs over, the one named last changes fastest.
Arguments:
- hidden: bfloat16 [64, 2048], P('mlp'), may hold values from -6 to 6
- lengths: int32 [64], P('mlp'), may hold values from 4 to 8192, as said below
- attention_gain: bfloat16 [2048], replicated, may hold values from 0.099609375 to 1.8984375
- query_weight: bfloat16 [2048, 2048], P('seq', 'tp'), may hold values from -0.125 to 0.125
- key_weight: bfloat16 [2048, 512], P('seq', 'tp'), may hold values from -0.125 to 0.125
- value_weight: bfloat16 [2048, 512], P('seq', 'tp'), may hold values from -0.125 to 0.125
- cached_keys: bfloat16 [64, 8192, 512], P('mlp', 'seq', 'tp'), may hold values from -800 to 800
- cached_values: bfloat16 [64, 8192, 512], P('mlp', 'seq', 'tp'), may hold values from -8 to 8
- output_weight: bfloat16 [2048, 2048], P('tp', 'seq'), may hold values from -0.125 to 0.125
- feedforward_gain: bfloat16 [2048], replicated, may hold values from 0.099609375 to 1.8984375
- gate_weight: bfloat16 [2048, 8192], P('mlp', ('seq', 'tp')), may hold values from -0.125 to 0.125
- up_weight: bfloat16 [2048, 8192], P('mlp', ('seq', 'tp')), may hold values from -0.125 to 0.125
- down_weight: bfloat16 [8192, 2048], P(('seq', 'tp'), 'mlp'), may hold values from -0.0625 to 0.0625
Outputs:
- updated_hidden: bfloat16 [64, 2048], P('mlp')
- new_keys: bfloat16 [64, 512], P('mlp', 'tp')
- new_values: bfloat16 [64, 512], P('mlp', 'tp')
Inputs may be any that keep to these rules, and one draw needn't show every extreme that they name: `lengths`: one request in every draw has exactly 8192 cached tokens.
All inputs are finite; a program needn't handle non-finite values.
Results may differ from a plain program's by a relative error of at most 0.012.
Values may be sent and summed in bfloat16 or wider, within the bound.
No kernel may reach another device: no remote copies, remote signals or barrier semaphores. Data moves between devices by JAX's collectives and lax.ppermute only.
A program may use at most 64 MiB of HBM per device.

v0:
```python
import jax
import jax.numpy as jnp
from jax import lax
from jax.sharding import PartitionSpec as P

HD = 64


def rms_norm(vectors, weights):
    mean_square = jnp.mean(vectors * vectors, axis=-1, keepdims=True)
    return vectors * lax.rsqrt(mean_square + 1e-05) * weights.astype(jnp.float32)


def rotate(vectors, positions):
    half_dim = vectors.shape[-1] // 2
    inverse = 500000.0 ** (-(jnp.arange(half_dim, dtype=jnp.float32) * 2.0 / vectors.shape[-1]))
    angles = positions.astype(jnp.float32)[:, None] * inverse[None, :]
    cosine = jnp.cos(angles)[:, None, :]
    sine_part = jnp.sin(angles)[:, None, :]
    first_half = vectors[..., :half_dim]
    second_half = vectors[..., half_dim:]
    return jnp.concatenate(
        [
            first_half * cosine - second_half * sine_part,
            second_half * cosine + first_half * sine_part,
        ],
        axis=-1,
    )


def gathered_sum(x, axis):
    return jnp.sum(lax.all_gather(x, axis), axis=0)


def gather_blocks(x, axis):
    size = lax.axis_size(axis)
    me = lax.axis_index(axis)
    held = x[None]
    step = 1
    while step < size:
        other = lax.ppermute(held, axis, [(i, i ^ step) for i in range(size)])
        upper = me // step % 2 == 1
        held = jnp.where(
            upper, jnp.concatenate([other, held], axis=0), jnp.concatenate([held, other], axis=0)
        )
        step *= 2
    return held


def butterfly_sum(x, axis):
    size = lax.axis_size(axis)
    step = 1
    while step < size:
        pairs = [(i, i ^ step) for i in range(size)]
        x = x + lax.ppermute(x, axis, pairs)
        step *= 2
    return x


def per_device(
    hidden,
    lengths,
    attention_gain,
    query_weight,
    key_weight,
    value_weight,
    cached_keys,
    cached_values,
    output_weight,
    feedforward_gain,
    gate_weight,
    up_weight,
    down_weight,
):
    slab_rows, hidden_units = gate_weight.shape
    with jax.named_scope("mlp_weight_gather"):
        slab = jnp.stack(
            [gate_weight, up_weight, down_weight.reshape(slab_rows, hidden_units)], axis=0
        )
        blocks = gather_blocks(slab, "mlp")
    slabs = blocks.shape[0]
    gate_full = blocks[:, 0].reshape(slabs * slab_rows, hidden_units)
    up_full = blocks[:, 1].reshape(slabs * slab_rows, hidden_units)
    down_blocks = blocks[:, 2].reshape(slabs, hidden_units, slab_rows)
    requests = hidden.shape[0]
    stream = hidden.astype(jnp.float32)
    normed = rms_norm(stream, attention_gain).astype(jnp.bfloat16)
    column_width = query_weight.shape[0]
    own_columns = lax.dynamic_slice_in_dim(
        normed, lax.axis_index("seq") * column_width, column_width, 1
    )
    query_width = query_weight.shape[1]
    key_width = key_weight.shape[1]
    with jax.named_scope("qkv_projection"):
        partial = jnp.concatenate(
            [
                jnp.dot(own_columns, query_weight, preferred_element_type=jnp.float32),
                jnp.dot(own_columns, key_weight, preferred_element_type=jnp.float32),
                jnp.dot(own_columns, value_weight, preferred_element_type=jnp.float32),
            ],
            axis=1,
        )
        total = gathered_sum(partial, "seq")
    queries_raw = total[:, :query_width]
    keys_raw = total[:, query_width : query_width + key_width]
    values_raw = total[:, query_width + key_width :]
    local_heads = query_width // HD
    key_heads = key_width // HD
    group_size = local_heads // key_heads
    queries = rotate(queries_raw.reshape(requests, local_heads, HD), lengths).astype(jnp.bfloat16)
    new_keys = (
        rotate(keys_raw.reshape(requests, key_heads, HD), lengths)
        .reshape(requests, key_heads * HD)
        .astype(jnp.bfloat16)
    )
    new_values = values_raw.astype(jnp.bfloat16)
    grouped = queries.reshape(requests, key_heads, group_size, HD)
    block_span = cached_keys.shape[1]
    key_blocks = cached_keys.reshape(requests, block_span, key_heads, HD)
    value_blocks = cached_values.reshape(requests, block_span, key_heads, HD)
    score_scale = HD ** (-0.5)
    first_position = lax.axis_index("seq") * block_span
    positions = first_position + jnp.arange(block_span, dtype=jnp.int32)
    valid_mask = (positions[None, :] < lengths[:, None])[:, None, None, :]
    with jax.named_scope("local_attention"):
        scores = (
            jnp.einsum("rgqd,rpgd->rgqp", grouped, key_blocks, preferred_element_type=jnp.float32)
            * score_scale
        )
        block_max = jnp.max(jnp.where(valid_mask, scores, -1e30), axis=-1)
        exp_weights = jnp.where(valid_mask, jnp.exp(scores - block_max[..., None]), 0.0)
        block_sum = jnp.sum(exp_weights, axis=-1)
        block_acc = jnp.einsum(
            "rgqp,rpgd->rgqd",
            exp_weights.astype(jnp.bfloat16),
            value_blocks,
            preferred_element_type=jnp.float32,
        )
    with jax.named_scope("softmax_merge"):
        state = jnp.concatenate([block_max[..., None], block_sum[..., None], block_acc], axis=-1)
        every_state = lax.all_gather(state, "seq")
        every_max = every_state[..., 0]
        every_sum = every_state[..., 1]
        every_acc = every_state[..., 2:]
        query_float = grouped.astype(jnp.float32)
        self_score = (
            jnp.sum(
                query_float * new_keys.astype(jnp.float32).reshape(requests, key_heads, 1, HD),
                axis=-1,
            )
            * score_scale
        )
        overall_max = jnp.maximum(jnp.max(every_max, axis=0), self_score)
        rescale = jnp.exp(every_max - overall_max[None])
        self_weight = jnp.exp(self_score - overall_max)
        total_weight = jnp.sum(every_sum * rescale, axis=0) + self_weight
        weighted_sum = jnp.sum(every_acc * rescale[..., None], axis=0) + self_weight[
            ..., None
        ] * new_values.astype(jnp.float32).reshape(requests, key_heads, 1, HD)
        attended = (
            (weighted_sum / total_weight[..., None])
            .reshape(requests, local_heads * HD)
            .astype(jnp.bfloat16)
        )
    with jax.named_scope("output_projection"):
        partial_output = jnp.dot(attended, output_weight, preferred_element_type=jnp.float32)
        projected = lax.psum(partial_output, "tp").astype(jnp.bfloat16)
        projected = lax.all_gather(projected, "seq", axis=1, tiled=True)
    mixed_stream = stream + projected.astype(jnp.float32)
    mlp_input = rms_norm(mixed_stream, feedforward_gain).astype(jnp.bfloat16)
    with jax.named_scope("feed_forward"):
        gate = jnp.dot(mlp_input, gate_full, preferred_element_type=jnp.float32)
        upward = jnp.dot(mlp_input, up_full, preferred_element_type=jnp.float32)
        activated = (jax.nn.silu(gate) * upward).astype(jnp.bfloat16)
        down_part = jnp.einsum(
            "rh,jhc->rjc", activated, down_blocks, preferred_element_type=jnp.float32
        ).reshape(requests, slabs * slab_rows)
    with jax.named_scope("down_reduction"):
        down_total = butterfly_sum(gathered_sum(down_part, "tp"), "seq").astype(jnp.bfloat16)
    updated_hidden = (mixed_stream + down_total.astype(jnp.float32)).astype(jnp.bfloat16)
    return (updated_hidden, new_keys, new_values)


def solution(mesh):
    return jax.shard_map(
        per_device,
        mesh=mesh,
        in_specs=(
            P("mlp", None),
            P("mlp"),
            P(),
            P("seq", "tp"),
            P("seq", "tp"),
            P("seq", "tp"),
            P("mlp", "seq", "tp"),
            P("mlp", "seq", "tp"),
            P("tp", "seq"),
            P(),
            P("mlp", ("seq", "tp")),
            P("mlp", ("seq", "tp")),
            P(("seq", "tp"), "mlp"),
        ),
        out_specs=(P("mlp", None), P("mlp", "tp"), P("mlp", "tp")),
        check_vma=False,
    )
```

profile of v0, /device:TPU:64, one launch (start us, length us, event | category | flops | bytes accessed | tf_op | source)
XLA Modules:
  0.0 163.4 jit_solution(15652032731097320502)
XLA Ops:
  0.7 1.0 reshape.177
  1.6 0.9 maximum_bitcast_fusion
  2.5 3.5 %collective-permute-start = (bf16[1,3,256,128]{3,2,1,0:T(8,128)(2,1)S(1)}, bf16[1,3,256,128]{3,2,1,0:T(8,128)(2,1)}, u32[]{:S(2)}, u32[]{:S(2)}) collective-permute-start(bf16[1,3,256,128]{3,2,1,0:T(8,128)(2,1)S(1)} %maximum_bitcast_fusion), channel_id=1, source_target_pairs={{0,4},{4,0},{8,12},{12,8},{16,20},{20,16},{24,28},{28,24},{1,5},{5... | collective-permute-start | bytes 589832 | tf_op jit(solution)/shard_map/mlp_weight_gather/ppermute | solution.py:41
  6.8 0.9 multiply_reduce_fusion.1
  8.7 0.9 fusion.24
  9.6 1.0 fusion.28
  10.6 21.2 %all-gather = f32[128,768]{1,0:T(8,128)S(1)} all-gather(f32[8,768]{1,0:T(8,128)S(1)} %pad_maximum_fusion.1), channel_id=2, replica_groups=mesh['seq'=16,'mlp'=8,'tp'=4] {'seq'}, dimensions={0}, use_global_device_ids=true | all-gather | bytes 417792 | tf_op jit(solution)/shard_map/qkv_projection/all_gather | solution.py:32
  34.9 18.2 %all-gather.1 = f32[128,2,4,66]{3,2,1,0:T(4,128)S(1)} all-gather(f32[8,2,4,66]{3,2,1,0:T(4,128)S(1)} %pad_maximum_fusion), channel_id=3, replica_groups=mesh['seq'=16,'mlp'=8,'tp'=4] {'seq'}, dimensions={0}, use_global_device_ids=true | all-gather | bytes 287232 | tf_op jit(solution)/shard_map/softmax_merge/all_gather | solution.py:141
  55.4 1.1 maximum_select_fusion.2
  56.6 4.5 %collective-permute-start.1 = (bf16[2,3,256,128]{3,2,1,0:T(8,128)(2,1)S(1)}, bf16[2,3,256,128]{3,2,1,0:T(8,128)(2,1)S(1)}, u32[]{:S(2)}, u32[]{:S(2)}) collective-permute-start(bf16[2,3,256,128]{3,2,1,0:T(8,128)(2,1)S(1)} %maximum_select_fusion.2), channel_id=1, source_target_pairs={{0,8},{4,12},{8,0},{12,4},{16,24},{20,28},{24,16},{28,20},{1,9},{5... | collective-permute-start | bytes 1179656 | tf_op jit(solution)/shard_map/mlp_weight_gather/ppermute | solution.py:41
  61.8 17.2 %collective-permute-done.1 = bf16[2,3,256,128]{3,2,1,0:T(8,128)(2,1)S(1)} collective-permute-done((bf16[2,3,256,128]{3,2,1,0:T(8,128)(2,1)S(1)}, bf16[2,3,256,128]{3,2,1,0:T(8,128)(2,1)S(1)}, u32[]{:S(2)}, u32[]{:S(2)}) %collective-permute-start.1) | collective-permute-done | bytes 393248 | tf_op jit(solution)/shard_map/mlp_weight_gather/ppermute | solution.py:41
  79.2 6.9 %collective-permute-start.2 = (bf16[4,3,256,128]{3,2,1,0:T(8,128)(2,1)S(1)}, bf16[4,3,256,128]{3,2,1,0:T(8,128)(2,1)S(1)}, u32[]{:S(2)}, u32[]{:S(2)}) collective-permute-start(bf16[4,3,256,128]{3,2,1,0:T(8,128)(2,1)S(1)} %maximum_select_fusion.1), channel_id=1, source_target_pairs={{0,16},{4,20},{8,24},{12,28},{16,0},{20,4},{24,8},{28,12},{1,17},{... | collective-permute-start | bytes 2359304 | tf_op jit(solution)/shard_map/mlp_weight_gather/ppermute | solution.py:41
  86.5 10.5 %psum.7 = bf16[8,128]{1,0:T(8,128)(2,1)S(1)} all-reduce(f32[8,128]{1,0:T(8,128)S(1)} %fusion.30), channel_id=1, replica_groups=mesh['seq'=16,'mlp'=8,'tp'=4] {'tp'}, use_global_device_ids=true, to_apply=%region_8.9 | all-reduce | flops 1024 | bytes 6144 | tf_op jit(solution)/shard_map/output_projection/psum | solution.py:167
  96.9 14.5 %all_gather.22 = bf16[8,2048]{1,0:T(8,128)(2,1)S(1)} all-gather(bf16[8,128]{1,0:T(8,128)(2,1)S(1)} %psum.7), channel_id=1, replica_groups=mesh['seq'=16,'mlp'=8,'tp'=4] {'seq'}, dimensions={1}, use_global_device_ids=true | all-gather | bytes 34816 | tf_op jit(solution)/shard_map/output_projection/all_gather | solution.py:168
  111.6 9.9 %collective-permute-done.2 = bf16[4,3,256,128]{3,2,1,0:T(8,128)(2,1)S(1)} collective-permute-done((bf16[4,3,256,128]{3,2,1,0:T(8,128)(2,1)S(1)}, bf16[4,3,256,128]{3,2,1,0:T(8,128)(2,1)S(1)}, u32[]{:S(2)}, u32[]{:S(2)}) %collective-permute-start.2) | collective-permute-done | bytes 786464 | tf_op jit(solution)/shard_map/mlp_weight_gather/ppermute | solution.py:41
  123.0 12.6 %all-gather.2 = f32[32,2048]{1,0:T(8,128)S(1)} all-gather(f32[8,2048]{1,0:T(8,128)S(1)} %fusion.13), channel_id=4, replica_groups=mesh['seq'=16,'mlp'=8,'tp'=4] {'tp'}, dimensions={0}, use_global_device_ids=true | all-gather | bytes 327680 | tf_op jit(solution)/shard_map/down_reduction/all_gather | solution.py:32
  135.6 1.9 %collective-permute-start.3 = (f32[8,2048]{1,0:T(8,128)S(1)}, f32[8,2048]{1,0:T(8,128)S(1)}, u32[]{:S(2)}, u32[]{:S(2)}) collective-permute-start(f32[8,2048]{1,0:T(8,128)S(1)} %bitcast_reduce_fusion.1), channel_id=1, source_target_pairs={{0,32},{32,0},{64,96},{96,64},{128,160},{160,128},{192,224},{224,1... | collective-permute-start | bytes 196616 | tf_op jit(solution)/shard_map/down_reduction/ppermute | solution.py:55
  137.6 1.2 collective-permute-done.3
  138.8 2.3 %collective-permute-start.4 = (f32[8,2048]{1,0:T(8,128)S(1)}, f32[8,2048]{1,0:T(8,128)S(1)}, u32[]{:S(2)}, u32[]{:S(2)}) collective-permute-start(f32[8,2048]{1,0:T(8,128)S(1)} %add.98), channel_id=1, source_target_pairs={{0,64},{32,96},{64,0},{96,32},{128,192},{160,224},{192,128},{224,1... | collective-permute-start | bytes 196616 | tf_op jit(solution)/shard_map/down_reduction/ppermute | solution.py:55
  141.1 3.9 %collective-permute-done.4 = f32[8,2048]{1,0:T(8,128)S(1)} collective-permute-done((f32[8,2048]{1,0:T(8,128)S(1)}, f32[8,2048]{1,0:T(8,128)S(1)}, u32[]{:S(2)}, u32[]{:S(2)}) %collective-permute-start.4) | collective-permute-done | bytes 65568 | tf_op jit(solution)/shard_map/down_reduction/ppermute | solution.py:55
  145.0 2.2 %collective-permute-start.5 = (f32[8,2048]{1,0:T(8,128)S(1)}, f32[8,2048]{1,0:T(8,128)S(1)}, u32[]{:S(2)}, u32[]{:S(2)}) collective-permute-start(f32[8,2048]{1,0:T(8,128)S(1)} %add.99), channel_id=1, source_target_pairs={{0,128},{32,160},{64,192},{96,224},{128,0},{160,32},{192,64},{224,... | collective-permute-start | bytes 196616 | tf_op jit(solution)/shard_map/down_reduction/ppermute | solution.py:55
  147.1 4.9 %collective-permute-done.5 = f32[8,2048]{1,0:T(8,128)S(1)} collective-permute-done((f32[8,2048]{1,0:T(8,128)S(1)}, f32[8,2048]{1,0:T(8,128)S(1)}, u32[]{:S(2)}, u32[]{:S(2)}) %collective-permute-start.5) | collective-permute-done | bytes 65568 | tf_op jit(solution)/shard_map/down_reduction/ppermute | solution.py:55
  152.0 3.4 %collective-permute-start.6 = (f32[8,2048]{1,0:T(8,128)S(1)}, f32[8,2048]{1,0:T(8,128)S(1)}, u32[]{:S(2)}, u32[]{:S(2)}) collective-permute-start(f32[8,2048]{1,0:T(8,128)S(1)} %add.100), channel_id=1, source_target_pairs={{0,256},{32,288},{64,320},{96,352},{128,384},{160,416},{192,448},{... | collective-permute-start | bytes 196616 | tf_op jit(solution)/shard_map/down_reduction/ppermute | solution.py:55
  156.1 6.7 %collective-permute-done.6 = f32[8,2048]{1,0:T(8,128)S(1)} collective-permute-done((f32[8,2048]{1,0:T(8,128)S(1)}, f32[8,2048]{1,0:T(8,128)S(1)}, u32[]{:S(2)}, u32[]{:S(2)}) %collective-permute-start.6) | collective-permute-done | bytes 65568 | tf_op jit(solution)/shard_map/down_reduction/ppermute | solution.py:55
  (83 shorter events, 11.1 us)
Async XLA Ops:
  0.6 7.8 %copy-start = (bf16[128,512]{1,0:T(8,128)(2,1)S(1)}, bf16[128,512]{1,0:T(8,128)(2,1)}, u32[]{:S(2)}) copy-start(bf16[128,512]{1,0:T(8,128)(2,1)} %param.16) | copy-start | bytes 393220
  0.6 31.3 %copy-start.9 = (s32[8]{0:T(128)S(1)}, s32[8]{0:T(128)}, u32[]{:S(2)}) copy-start(s32[8]{0:T(128)} %param.14) | copy-start | bytes 100
  0.7 31.4 %copy-start.2 = (bf16[8,512,128]{2,1,0:T(8,128)(2,1)S(1)}, bf16[8,512,128]{2,1,0:T(8,128)(2,1)}, u32[]{:S(2)}) copy-start(bf16[8,512,128]{2,1,0:T(8,128)(2,1)} %param.19) | copy-start | bytes 3145732
  2.5 52.9 %collective-permute-start = (bf16[1,3,256,128]{3,2,1,0:T(8,128)(2,1)S(1)}, bf16[1,3,256,128]{3,2,1,0:T(8,128)(2,1)}, u32[]{:S(2)}, u32[]{:S(2)}) collective-permute-start(bf16[1,3,256,128]{3,2,1,0:T(8,128)(2,1)S(1)} %maximum_bitcast_fusion), channel_id=1, source_target_pairs={{0,4},{4,0},{8,12},{12,8},{16,20},{20,16},{24,28},{28,24},{1,5},{5... | collective-permute-start | bytes 589832 | tf_op jit(solution)/shard_map/mlp_weight_gather/ppermute | solution.py:41
  9.6 23.0 %copy-start.3 = (bf16[8,512,128]{2,1,0:T(8,128)(2,1)S(1)}, bf16[8,512,128]{2,1,0:T(8,128)(2,1)}, u32[]{:S(2)}) copy-start(bf16[8,512,128]{2,1,0:T(8,128)(2,1)} %param.20) | copy-start | bytes 3145732
  31.8 1.3 copy-start.5
  53.2 0.7 slice-start
  53.8 7.4 %copy-start.6 = (f32[8,768]{1,0:T(8,128)S(1)}, f32[8,768]{1,0:T(8,128)}, u32[]{:S(2)}) copy-start(f32[8,768]{1,0:T(8,128)} %copy-done.5) | copy-start | bytes 73732
  55.4 30.9 %copy-start.8 = (bf16[2048]{0:T(1024)(128)(2,1)S(1)}, bf16[2048]{0:T(1024)(128)(2,1)}, u32[]{:S(2)}) copy-start(bf16[2048]{0:T(1024)(128)(2,1)} %param.22) | copy-start | bytes 12292
  55.4 30.9 %copy-start.4 = (bf16[512,128]{1,0:T(8,128)(2,1)S(1)}, bf16[512,128]{1,0:T(8,128)(2,1)}, u32[]{:S(2)}) copy-start(bf16[512,128]{1,0:T(8,128)(2,1)} %param.21) | copy-start | bytes 393220
  56.5 54.9 %copy-start.1 = (bf16[8,2048]{1,0:T(8,128)(2,1)S(1)}, bf16[8,2048]{1,0:T(8,128)(2,1)}, u32[]{:S(2)}) copy-start(bf16[8,2048]{1,0:T(8,128)(2,1)} %param.13) | copy-start | bytes 98308
  56.6 22.5 %collective-permute-start.1 = (bf16[2,3,256,128]{3,2,1,0:T(8,128)(2,1)S(1)}, bf16[2,3,256,128]{3,2,1,0:T(8,128)(2,1)S(1)}, u32[]{:S(2)}, u32[]{:S(2)}) collective-permute-start(bf16[2,3,256,128]{3,2,1,0:T(8,128)(2,1)S(1)} %maximum_select_fusion.2), channel_id=1, source_target_pairs={{0,8},{4,12},{8,0},{12,4},{16,24},{20,28},{24,16},{28,20},{1,9},{5... | collective-permute-start | bytes 1179656 | tf_op jit(solution)/shard_map/mlp_weight_gather/ppermute | solution.py:41
  61.3 60.5 %copy-start.7 = (bf16[8,128]{1,0:T(8,128)(2,1)}, bf16[8,128]{1,0:T(8,128)(2,1)S(1)}, u32[]{:S(2)}) copy-start(bf16[8,128]{1,0:T(8,128)(2,1)S(1)} %slice.79) | copy-start | bytes 6148
  79.2 42.3 %collective-permute-start.2 = (bf16[4,3,256,128]{3,2,1,0:T(8,128)(2,1)S(1)}, bf16[4,3,256,128]{3,2,1,0:T(8,128)(2,1)S(1)}, u32[]{:S(2)}, u32[]{:S(2)}) collective-permute-start(bf16[4,3,256,128]{3,2,1,0:T(8,128)(2,1)S(1)} %maximum_select_fusion.1), channel_id=1, source_target_pairs={{0,16},{4,20},{8,24},{12,28},{16,0},{20,4},{24,8},{28,12},{1,17},{... | collective-permute-start | bytes 2359304 | tf_op jit(solution)/shard_map/mlp_weight_gather/ppermute | solution.py:41
  135.6 3.1 %collective-permute-start.3 = (f32[8,2048]{1,0:T(8,128)S(1)}, f32[8,2048]{1,0:T(8,128)S(1)}, u32[]{:S(2)}, u32[]{:S(2)}) collective-permute-start(f32[8,2048]{1,0:T(8,128)S(1)} %bitcast_reduce_fusion.1), channel_id=1, source_target_pairs={{0,32},{32,0},{64,96},{96,64},{128,160},{160,128},{192,224},{224,1... | collective-permute-start | bytes 196616 | tf_op jit(solution)/shard_map/down_reduction/ppermute | solution.py:55
  138.8 6.2 %collective-permute-start.4 = (f32[8,2048]{1,0:T(8,128)S(1)}, f32[8,2048]{1,0:T(8,128)S(1)}, u32[]{:S(2)}, u32[]{:S(2)}) collective-permute-start(f32[8,2048]{1,0:T(8,128)S(1)} %add.98), channel_id=1, source_target_pairs={{0,64},{32,96},{64,0},{96,32},{128,192},{160,224},{192,128},{224,1... | collective-permute-start | bytes 196616 | tf_op jit(solution)/shard_map/down_reduction/ppermute | solution.py:55
  145.0 7.1 %collective-permute-start.5 = (f32[8,2048]{1,0:T(8,128)S(1)}, f32[8,2048]{1,0:T(8,128)S(1)}, u32[]{:S(2)}, u32[]{:S(2)}) collective-permute-start(f32[8,2048]{1,0:T(8,128)S(1)} %add.99), channel_id=1, source_target_pairs={{0,128},{32,160},{64,192},{96,224},{128,0},{160,32},{192,64},{224,... | collective-permute-start | bytes 196616 | tf_op jit(solution)/shard_map/down_reduction/ppermute | solution.py:55
  152.0 10.8 %collective-permute-start.6 = (f32[8,2048]{1,0:T(8,128)S(1)}, f32[8,2048]{1,0:T(8,128)S(1)}, u32[]{:S(2)}, u32[]{:S(2)}) collective-permute-start(f32[8,2048]{1,0:T(8,128)S(1)} %add.100), channel_id=1, source_target_pairs={{0,256},{32,288},{64,320},{96,352},{128,384},{160,416},{192,448},{... | collective-permute-start | bytes 196616 | tf_op jit(solution)/shard_map/down_reduction/ppermute | solution.py:55
where the time goes:
time: 164 us; the launch traced here: 163 us
  blocking collectives  77 us (47%)
  waiting for transfers between devices  43.8 us (27%)
  starting transfers between devices  24.6 us (15%)
  other arithmetic  6.82 us (4%)
  local copies, waits for them, and re-layouts  6.29 us (4%)
  matrix products  3.79 us (2%)
    all_gather x2, blocking collectives, gathered_sum(): return jnp.sum(lax.all_gather(x, axis), axis=0)  33.8 us
    ppermute x3, waiting for transfers between devices, gather_blocks(): other = lax.ppermute(held, axis, [(i, i ^ step) for i in range(size)])  27.1 us
    all_gather x1, blocking collectives, per_device(): every_state = lax.all_gather(state, 'seq')  18.2 us
    ppermute x4, waiting for transfers between devices, butterfly_sum(): x = x + lax.ppermute(x, axis, pairs)  16.8 us
    ppermute x3, starting transfers between devices, gather_blocks(): other = lax.ppermute(held, axis, [(i, i ^ step) for i in range(size)])  14.9 us
    all_gather x1, blocking collectives, per_device(): projected = lax.all_gather(projected, 'seq', axis=1, tiled=True)  14.5 us
    psum x1, blocking collectives, per_device(): projected = lax.psum(partial_output, 'tp').astype(jnp.bfloat16)  10.5 us
    ppermute x4, starting transfers between devices, butterfly_sum(): x = x + lax.ppermute(x, axis, pairs)  9.69 us
  transfers between devices with their start and end apart: 7, of which 6 were waited for; matrix products, arithmetic and copies ran while one was open for 7% of the time, Pallas kernels for 0%

commit v1 on v0

--- a/solution.py
+++ b/solution.py
@@ -164,7 +164,8 @@
         )
     with jax.named_scope("output_projection"):
         partial_output = jnp.dot(attended, output_weight, preferred_element_type=jnp.float32)
-        projected = lax.psum(partial_output, "tp").astype(jnp.bfloat16)
+        series_divide = lambda v0: jnp.sum(lax.all_gather(v0, "tp"), axis=0)
+        projected = series_divide(partial_output).astype(jnp.bfloat16)
         projected = lax.all_gather(projected, "seq", axis=1, tiled=True)
     mixed_stream = stream + projected.astype(jnp.float32)
     mlp_input = rms_norm(mixed_stream, feedforward_gain).astype(jnp.bfloat16)

time: 164 us -> 164 us (level)
  blocking collectives: 77 us -> 78.9 us
  waiting for transfers between devices: 43.8 us -> 41.9 us
    all_gather x0 -> x1, blocking collectives: none -> 12.4 us  [per_device(): series_divide = lambda v0: jnp.sum(lax.all_gather(v0, 'tp'), axis=0)]
    psum x1 -> x0, blocking collectives: 10.5 us -> none  [per_device(): projected = lax.psum(partial_output, 'tp').astype(jnp.bfloat16)]
    ppermute x3, waiting for transfers between devices: 27.1 us -> 25.2 us  [gather_blocks(): other = lax.ppermute(held, axis, [(i, i ^ step) for i in range(size)])]
where the time goes in v1:
time: 164 us; the launch traced here: 163 us
  blocking collectives  78.9 us (48%)
  waiting for transfers between devices  41.9 us (26%)
  starting transfers between devices  24.6 us (15%)
  other arithmetic  6.83 us (4%)
  local copies, waits for them, and re-layouts  6.29 us (4%)
  matrix products  3.79 us (2%)
    all_gather x2, blocking collectives, gathered_sum(): return jnp.sum(lax.all_gather(x, axis), axis=0)  33.8 us
    ppermute x3, waiting for transfers between devices, gather_blocks(): other = lax.ppermute(held, axis, [(i, i ^ step) for i in range(size)])  25.2 us
    all_gather x1, blocking collectives, per_device(): every_state = lax.all_gather(state, 'seq')  18.2 us
    ppermute x4, waiting for transfers between devices, butterfly_sum(): x = x + lax.ppermute(x, axis, pairs)  16.8 us
    ppermute x3, starting transfers between devices, gather_blocks(): other = lax.ppermute(held, axis, [(i, i ^ step) for i in range(size)])  14.9 us
    all_gather x1, blocking collectives, per_device(): projected = lax.all_gather(projected, 'seq', axis=1, tiled=True)  14.5 us
    all_gather x1, blocking collectives, per_device(): series_divide = lambda v0: jnp.sum(lax.all_gather(v0, 'tp'), axis=0)  12.4 us
    ppermute x4, starting transfers between devices, butterfly_sum(): x = x + lax.ppermute(x, axis, pairs)  9.69 us
  transfers between devices with their start and end apart: 7, of which 6 were waited for; matrix products, arithmetic and copies ran while one was open for 7% of the time, Pallas kernels for 0%

profile of v1, /device:TPU:64, one launch (start us, length us, event | category | flops | bytes accessed | tf_op | source)
XLA Modules:
  0.0 163.4 jit_solution(13436895314683782846)
XLA Ops:
  0.7 1.0 reshape.177
  1.6 0.9 maximum_bitcast_fusion
  2.5 3.5 %collective-permute-start = (bf16[1,3,256,128]{3,2,1,0:T(8,128)(2,1)S(1)}, bf16[1,3,256,128]{3,2,1,0:T(8,128)(2,1)}, u32[]{:S(2)}, u32[]{:S(2)}) collective-permute-start(bf16[1,3,256,128]{3,2,1,0:T(8,128)(2,1)S(1)} %maximum_bitcast_fusion), channel_id=1, source_target_pairs={{0,4},{4,0},{8,12},{12,8},{16,20},{20,16},{24,28},{28,24},{1,5},{5... | collective-permute-start | bytes 589832 | tf_op jit(solution)/shard_map/mlp_weight_gather/ppermute | solution.py:41
  6.8 0.9 multiply_reduce_fusion.1
  8.7 0.9 fusion.24
  9.6 1.0 fusion.28
  10.6 21.2 %all-gather = f32[128,768]{1,0:T(8,128)S(1)} all-gather(f32[8,768]{1,0:T(8,128)S(1)} %pad_maximum_fusion.1), channel_id=2, replica_groups=mesh['seq'=16,'mlp'=8,'tp'=4] {'seq'}, dimensions={0}, use_global_device_ids=true | all-gather | bytes 417792 | tf_op jit(solution)/shard_map/qkv_projection/all_gather | solution.py:32
  34.9 18.2 %all-gather.1 = f32[128,2,4,66]{3,2,1,0:T(4,128)S(1)} all-gather(f32[8,2,4,66]{3,2,1,0:T(4,128)S(1)} %pad_maximum_fusion), channel_id=3, replica_groups=mesh['seq'=16,'mlp'=8,'tp'=4] {'seq'}, dimensions={0}, use_global_device_ids=true | all-gather | bytes 287232 | tf_op jit(solution)/shard_map/softmax_merge/all_gather | solution.py:141
  55.4 1.1 maximum_select_fusion.2
  56.6 4.5 %collective-permute-start.1 = (bf16[2,3,256,128]{3,2,1,0:T(8,128)(2,1)S(1)}, bf16[2,3,256,128]{3,2,1,0:T(8,128)(2,1)S(1)}, u32[]{:S(2)}, u32[]{:S(2)}) collective-permute-start(bf16[2,3,256,128]{3,2,1,0:T(8,128)(2,1)S(1)} %maximum_select_fusion.2), channel_id=1, source_target_pairs={{0,8},{4,12},{8,0},{12,4},{16,24},{20,28},{24,16},{28,20},{1,9},{5... | collective-permute-start | bytes 1179656 | tf_op jit(solution)/shard_map/mlp_weight_gather/ppermute | solution.py:41
  61.8 17.2 %collective-permute-done.1 = bf16[2,3,256,128]{3,2,1,0:T(8,128)(2,1)S(1)} collective-permute-done((bf16[2,3,256,128]{3,2,1,0:T(8,128)(2,1)S(1)}, bf16[2,3,256,128]{3,2,1,0:T(8,128)(2,1)S(1)}, u32[]{:S(2)}, u32[]{:S(2)}) %collective-permute-start.1) | collective-permute-done | bytes 393248 | tf_op jit(solution)/shard_map/mlp_weight_gather/ppermute | solution.py:41
  79.2 6.9 %collective-permute-start.2 = (bf16[4,3,256,128]{3,2,1,0:T(8,128)(2,1)S(1)}, bf16[4,3,256,128]{3,2,1,0:T(8,128)(2,1)S(1)}, u32[]{:S(2)}, u32[]{:S(2)}) collective-permute-start(bf16[4,3,256,128]{3,2,1,0:T(8,128)(2,1)S(1)} %maximum_select_fusion.1), channel_id=1, source_target_pairs={{0,16},{4,20},{8,24},{12,28},{16,0},{20,4},{24,8},{28,12},{1,17},{... | collective-permute-start | bytes 2359304 | tf_op jit(solution)/shard_map/mlp_weight_gather/ppermute | solution.py:41
  86.5 12.4 %all-gather.2 = f32[32,128]{1,0:T(8,128)S(1)} all-gather(f32[8,128]{1,0:T(8,128)S(1)} %fusion.30), channel_id=4, replica_groups=mesh['seq'=16,'mlp'=8,'tp'=4] {'tp'}, dimensions={0}, use_global_device_ids=true | all-gather | bytes 20480 | tf_op jit(solution)/shard_map/output_projection/all_gather | solution.py:167
  98.9 14.5 %all_gather.30 = bf16[8,2048]{1,0:T(8,128)(2,1)S(1)} all-gather(bf16[8,128]{1,0:T(8,128)(2,1)S(1)} %bitcast_reduce_fusion.2), channel_id=1, replica_groups=mesh['seq'=16,'mlp'=8,'tp'=4] {'seq'}, dimensions={1}, use_global_device_ids=true | all-gather | bytes 34816 | tf_op jit(solution)/shard_map/output_projection/all_gather | solution.py:169
  113.5 8.0 %collective-permute-done.2 = bf16[4,3,256,128]{3,2,1,0:T(8,128)(2,1)S(1)} collective-permute-done((bf16[4,3,256,128]{3,2,1,0:T(8,128)(2,1)S(1)}, bf16[4,3,256,128]{3,2,1,0:T(8,128)(2,1)S(1)}, u32[]{:S(2)}, u32[]{:S(2)}) %collective-permute-start.2) | collective-permute-done | bytes 786464 | tf_op jit(solution)/shard_map/mlp_weight_gather/ppermute | solution.py:41
  123.0 12.6 %all-gather.3 = f32[32,2048]{1,0:T(8,128)S(1)} all-gather(f32[8,2048]{1,0:T(8,128)S(1)} %fusion.13), channel_id=5, replica_groups=mesh['seq'=16,'mlp'=8,'tp'=4] {'tp'}, dimensions={0}, use_global_device_ids=true | all-gather | bytes 327680 | tf_op jit(solution)/shard_map/down_reduction/all_gather | solution.py:32
  135.6 1.9 %collective-permute-start.3 = (f32[8,2048]{1,0:T(8,128)S(1)}, f32[8,2048]{1,0:T(8,128)S(1)}, u32[]{:S(2)}, u32[]{:S(2)}) collective-permute-start(f32[8,2048]{1,0:T(8,128)S(1)} %bitcast_reduce_fusion.1), channel_id=1, source_target_pairs={{0,32},{32,0},{64,96},{96,64},{128,160},{160,128},{192,224},{224,1... | collective-permute-start | bytes 196616 | tf_op jit(solution)/shard_map/down_reduction/ppermute | solution.py:55
  137.6 1.2 collective-permute-done.3
  138.8 2.3 %collective-permute-start.4 = (f32[8,2048]{1,0:T(8,128)S(1)}, f32[8,2048]{1,0:T(8,128)S(1)}, u32[]{:S(2)}, u32[]{:S(2)}) collective-permute-start(f32[8,2048]{1,0:T(8,128)S(1)} %add.96), channel_id=1, source_target_pairs={{0,64},{32,96},{64,0},{96,32},{128,192},{160,224},{192,128},{224,1... | collective-permute-start | bytes 196616 | tf_op jit(solution)/shard_map/down_reduction/ppermute | solution.py:55
  141.1 3.9 %collective-permute-done.4 = f32[8,2048]{1,0:T(8,128)S(1)} collective-permute-done((f32[8,2048]{1,0:T(8,128)S(1)}, f32[8,2048]{1,0:T(8,128)S(1)}, u32[]{:S(2)}, u32[]{:S(2)}) %collective-permute-start.4) | collective-permute-done | bytes 65568 | tf_op jit(solution)/shard_map/down_reduction/ppermute | solution.py:55
  145.0 2.2 %collective-permute-start.5 = (f32[8,2048]{1,0:T(8,128)S(1)}, f32[8,2048]{1,0:T(8,128)S(1)}, u32[]{:S(2)}, u32[]{:S(2)}) collective-permute-start(f32[8,2048]{1,0:T(8,128)S(1)} %add.97), channel_id=1, source_target_pairs={{0,128},{32,160},{64,192},{96,224},{128,0},{160,32},{192,64},{224,... | collective-permute-start | bytes 196616 | tf_op jit(solution)/shard_map/down_reduction/ppermute | solution.py:55
  147.1 4.9 %collective-permute-done.5 = f32[8,2048]{1,0:T(8,128)S(1)} collective-permute-done((f32[8,2048]{1,0:T(8,128)S(1)}, f32[8,2048]{1,0:T(8,128)S(1)}, u32[]{:S(2)}, u32[]{:S(2)}) %collective-permute-start.5) | collective-permute-done | bytes 65568 | tf_op jit(solution)/shard_map/down_reduction/ppermute | solution.py:55
  152.0 3.4 %collective-permute-start.6 = (f32[8,2048]{1,0:T(8,128)S(1)}, f32[8,2048]{1,0:T(8,128)S(1)}, u32[]{:S(2)}, u32[]{:S(2)}) collective-permute-start(f32[8,2048]{1,0:T(8,128)S(1)} %add.98), channel_id=1, source_target_pairs={{0,256},{32,288},{64,320},{96,352},{128,384},{160,416},{192,448},{... | collective-permute-start | bytes 196616 | tf_op jit(solution)/shard_map/down_reduction/ppermute | solution.py:55
  156.1 6.7 %collective-permute-done.6 = f32[8,2048]{1,0:T(8,128)S(1)} collective-permute-done((f32[8,2048]{1,0:T(8,128)S(1)}, f32[8,2048]{1,0:T(8,128)S(1)}, u32[]{:S(2)}, u32[]{:S(2)}) %collective-permute-start.6) | collective-permute-done | bytes 65568 | tf_op jit(solution)/shard_map/down_reduction/ppermute | solution.py:55
  (84 shorter events, 11.1 us)
Async XLA Ops:
  0.6 7.8 %copy-start = (bf16[128,512]{1,0:T(8,128)(2,1)S(1)}, bf16[128,512]{1,0:T(8,128)(2,1)}, u32[]{:S(2)}) copy-start(bf16[128,512]{1,0:T(8,128)(2,1)} %param.16) | copy-start | bytes 393220
  0.6 31.3 %copy-start.9 = (s32[8]{0:T(128)S(1)}, s32[8]{0:T(128)}, u32[]{:S(2)}) copy-start(s32[8]{0:T(128)} %param.14) | copy-start | bytes 100
  0.7 31.4 %copy-start.2 = (bf16[8,512,128]{2,1,0:T(8,128)(2,1)S(1)}, bf16[8,512,128]{2,1,0:T(8,128)(2,1)}, u32[]{:S(2)}) copy-start(bf16[8,512,128]{2,1,0:T(8,128)(2,1)} %param.19) | copy-start | bytes 3145732
  2.5 52.9 %collective-permute-start = (bf16[1,3,256,128]{3,2,1,0:T(8,128)(2,1)S(1)}, bf16[1,3,256,128]{3,2,1,0:T(8,128)(2,1)}, u32[]{:S(2)}, u32[]{:S(2)}) collective-permute-start(bf16[1,3,256,128]{3,2,1,0:T(8,128)(2,1)S(1)} %maximum_bitcast_fusion), channel_id=1, source_target_pairs={{0,4},{4,0},{8,12},{12,8},{16,20},{20,16},{24,28},{28,24},{1,5},{5... | collective-permute-start | bytes 589832 | tf_op jit(solution)/shard_map/mlp_weight_gather/ppermute | solution.py:41
  9.6 23.0 %copy-start.3 = (bf16[8,512,128]{2,1,0:T(8,128)(2,1)S(1)}, bf16[8,512,128]{2,1,0:T(8,128)(2,1)}, u32[]{:S(2)}) copy-start(bf16[8,512,128]{2,1,0:T(8,128)(2,1)} %param.20) | copy-start | bytes 3145732
  31.8 1.3 copy-start.5
  53.2 0.7 slice-start
  53.8 7.4 %copy-start.6 = (f32[8,768]{1,0:T(8,128)S(1)}, f32[8,768]{1,0:T(8,128)}, u32[]{:S(2)}) copy-start(f32[8,768]{1,0:T(8,128)} %copy-done.5) | copy-start | bytes 73732
  55.4 31.0 %copy-start.8 = (bf16[2048]{0:T(1024)(128)(2,1)S(1)}, bf16[2048]{0:T(1024)(128)(2,1)}, u32[]{:S(2)}) copy-start(bf16[2048]{0:T(1024)(128)(2,1)} %param.22) | copy-start | bytes 12292
  55.4 30.9 %copy-start.4 = (bf16[512,128]{1,0:T(8,128)(2,1)S(1)}, bf16[512,128]{1,0:T(8,128)(2,1)}, u32[]{:S(2)}) copy-start(bf16[512,128]{1,0:T(8,128)(2,1)} %param.21) | copy-start | bytes 393220
  56.5 56.8 %copy-start.1 = (bf16[8,2048]{1,0:T(8,128)(2,1)S(1)}, bf16[8,2048]{1,0:T(8,128)(2,1)}, u32[]{:S(2)}) copy-start(bf16[8,2048]{1,0:T(8,128)(2,1)} %param.13) | copy-start | bytes 98308
  56.6 22.5 %collective-permute-start.1 = (bf16[2,3,256,128]{3,2,1,0:T(8,128)(2,1)S(1)}, bf16[2,3,256,128]{3,2,1,0:T(8,128)(2,1)S(1)}, u32[]{:S(2)}, u32[]{:S(2)}) collective-permute-start(bf16[2,3,256,128]{3,2,1,0:T(8,128)(2,1)S(1)} %maximum_select_fusion.2), channel_id=1, source_target_pairs={{0,8},{4,12},{8,0},{12,4},{16,24},{20,28},{24,16},{28,20},{1,9},{5... | collective-permute-start | bytes 1179656 | tf_op jit(solution)/shard_map/mlp_weight_gather/ppermute | solution.py:41
  61.3 60.5 %copy-start.7 = (bf16[8,128]{1,0:T(8,128)(2,1)}, bf16[8,128]{1,0:T(8,128)(2,1)S(1)}, u32[]{:S(2)}) copy-start(bf16[8,128]{1,0:T(8,128)(2,1)S(1)} %slice.79) | copy-start | bytes 6148
  79.2 42.3 %collective-permute-start.2 = (bf16[4,3,256,128]{3,2,1,0:T(8,128)(2,1)S(1)}, bf16[4,3,256,128]{3,2,1,0:T(8,128)(2,1)S(1)}, u32[]{:S(2)}, u32[]{:S(2)}) collective-permute-start(bf16[4,3,256,128]{3,2,1,0:T(8,128)(2,1)S(1)} %maximum_select_fusion.1), channel_id=1, source_target_pairs={{0,16},{4,20},{8,24},{12,28},{16,0},{20,4},{24,8},{28,12},{1,17},{... | collective-permute-start | bytes 2359304 | tf_op jit(solution)/shard_map/mlp_weight_gather/ppermute | solution.py:41
  135.6 3.1 %collective-permute-start.3 = (f32[8,2048]{1,0:T(8,128)S(1)}, f32[8,2048]{1,0:T(8,128)S(1)}, u32[]{:S(2)}, u32[]{:S(2)}) collective-permute-start(f32[8,2048]{1,0:T(8,128)S(1)} %bitcast_reduce_fusion.1), channel_id=1, source_target_pairs={{0,32},{32,0},{64,96},{96,64},{128,160},{160,128},{192,224},{224,1... | collective-permute-start | bytes 196616 | tf_op jit(solution)/shard_map/down_reduction/ppermute | solution.py:55
  138.8 6.2 %collective-permute-start.4 = (f32[8,2048]{1,0:T(8,128)S(1)}, f32[8,2048]{1,0:T(8,128)S(1)}, u32[]{:S(2)}, u32[]{:S(2)}) collective-permute-start(f32[8,2048]{1,0:T(8,128)S(1)} %add.96), channel_id=1, source_target_pairs={{0,64},{32,96},{64,0},{96,32},{128,192},{160,224},{192,128},{224,1... | collective-permute-start | bytes 196616 | tf_op jit(solution)/shard_map/down_reduction/ppermute | solution.py:55
  145.0 7.1 %collective-permute-start.5 = (f32[8,2048]{1,0:T(8,128)S(1)}, f32[8,2048]{1,0:T(8,128)S(1)}, u32[]{:S(2)}, u32[]{:S(2)}) collective-permute-start(f32[8,2048]{1,0:T(8,128)S(1)} %add.97), channel_id=1, source_target_pairs={{0,128},{32,160},{64,192},{96,224},{128,0},{160,32},{192,64},{224,... | collective-permute-start | bytes 196616 | tf_op jit(solution)/shard_map/down_reduction/ppermute | solution.py:55
  152.0 10.8 %collective-permute-start.6 = (f32[8,2048]{1,0:T(8,128)S(1)}, f32[8,2048]{1,0:T(8,128)S(1)}, u32[]{:S(2)}, u32[]{:S(2)}) collective-permute-start(f32[8,2048]{1,0:T(8,128)S(1)} %add.98), channel_id=1, source_target_pairs={{0,256},{32,288},{64,320},{96,352},{128,384},{160,416},{192,448},{... | collective-permute-start | bytes 196616 | tf_op jit(solution)/shard_map/down_reduction/ppermute | solution.py:55
